TPU v7x, 128 devices: a whole 4x4x4 slice. The times are simulated.
128 devices in a mesh: mode: 8 (over x, core), member: 16 (over z, y).
Axes of the slice: x: 4, y: 4, z: 4, core: 2. Of those that a mesh axis runs over, the one named last changes fastest.
Arguments:
- ground_accel: bfloat16 [4, 639], replicated, may hold values from -6 to 6
- modal_kernel: bfloat16 [4096, 512], P(('mode', 'member')), may hold values from -0.25 to 0.25
- mode_shapes: bfloat16 [98304, 4096], P('member', 'mode'), may hold values from -0.09375 to 0.09375
- member_owner: int32 [16384, 1], P('member'), may hold values from 0 to 127; in each aligned block of 128 rows (0 to 127, 128 to 255, ...) at most 2 rows name the same one
- member_group: int32 [16384, 1], P('member'), may hold values from 0 to 3
- record_table: int32 [512, 8], P(('mode', 'member')), may hold values from 0 to 3
- case_coef: float32 [8, 6], replicated, may hold values from -1.5 to 1.5
- gravity: float32 [512, 8], P(('mode', 'member')), may hold values from -10 to 10
Outputs:
- demand: float32 [512, 8], P(('mode', 'member'))
Inputs may be any that keep to these rules, and one draw needn't show every extreme that they name: `member_owner`: in each aligned block of 1024 / 8 members no owner is named more than 2 times, a bound that some block reaches.
All inputs are finite; a program needn't handle non-finite values.
Results may differ from a plain program's by a relative error of at most 0.0065.
Values may be sent and summed in bfloat16 or wider, within the bound.
No kernel may reach another device: no remote copies, remote signals or barrier semaphores. Data moves between devices by JAX's collectives and lax.ppermute only.
A program may use at most 64 MiB of HBM per device.

v0:
```python
import jax
import jax.numpy as jnp
from jax import lax
from jax.sharding import PartitionSpec as P


def lagged_table(ground_accel, tap_count):
    record_count, span_len = ground_accel.shape
    step_count = span_len - tap_count + 1
    tiled = jnp.tile(ground_accel, (1, step_count + 1))[:, : step_count * (span_len + 1)]
    windows = tiled.reshape(record_count, step_count, span_len + 1)[:, :, :tap_count]
    return windows.reshape(record_count * step_count, tap_count)


def local(
    ground_accel,
    modal_kernel,
    mode_shapes,
    member_owner,
    member_group,
    record_table,
    case_coef,
    gravity,
):
    tap_count = modal_kernel.shape[1]
    record_count = ground_accel.shape[0]
    comp_count = case_coef.shape[1]
    n_mode = lax.axis_size("mode")
    n_member = lax.axis_size("member")
    groups_here = gravity.shape[0]
    group_total = groups_here * n_mode * n_member
    lagged = lagged_table(ground_accel, tap_count)
    local_resp = lax.dot_general(
        modal_kernel[:, ::-1], lagged, (((1,), (1,)), ((), ())), preferred_element_type=jnp.float32
    ).astype(jnp.bfloat16)
    modal_resp = lax.all_gather(local_resp, "member", axis=0, tiled=True)
    partial = jnp.dot(mode_shapes, modal_resp, preferred_element_type=jnp.float32).astype(
        jnp.bfloat16
    )
    members_here = member_owner.shape[0]
    packed = partial.reshape(members_here, comp_count * partial.shape[1])
    group_index = member_owner[:, 0] * groups_here + member_group[:, 0]
    selector = (jnp.arange(group_total)[:, None] == group_index[None, :]).astype(jnp.bfloat16)
    group_part = jnp.dot(selector, packed, preferred_element_type=jnp.float32)
    by_mode = lax.psum_scatter(
        group_part.astype(jnp.bfloat16), "mode", scatter_dimension=0, tiled=True
    )
    group_sums = lax.psum_scatter(
        by_mode.astype(jnp.float32), "member", scatter_dimension=0, tiled=True
    )
    group_sums = group_sums.reshape(groups_here, comp_count, record_count, -1)
    case_mix = jnp.einsum("sc,gcrt->gsrt", case_coef, group_sums, precision=lax.Precision.HIGHEST)
    record_pick = (record_table[:, :, None] == jnp.arange(record_count)[None, None, :]).astype(
        jnp.float32
    )
    selected = jnp.sum(record_pick[:, :, :, None] * case_mix, axis=2)
    combined = gravity[:, :, None] + selected
    return jnp.max(jnp.abs(combined), axis=2)


def solution(mesh):
    placed = (
        P(),
        P(("mode", "member"), None),
        P("member", "mode"),
        P("member", None),
        P("member", None),
        P(("mode", "member"), None),
        P(),
        P(("mode", "member"), None),
    )
    return jax.shard_map(
        local, mesh=mesh, in_specs=placed, out_specs=P(("mode", "member"), None), check_vma=False
    )
```

profile of v0, /device:TPU:0, one launch (start us, length us, event | category | flops | bytes accessed | tf_op | source)
XLA Modules:
  0.0 198.6 jit_solution(844657869856164750)
XLA Ops:
  6.5 0.0 copy-start
  6.5 0.0 reduce-scatter.2.cloned.1.call-start
  6.5 0.8 tile.4
  7.3 0.6 tile.10
  7.9 0.2 slice.8
  8.2 0.1 copy.21
  8.3 1.6 rev.3
  9.9 0.2 convolution_convert_fusion.2
  10.2 25.6 %all_gather.3 = bf16[512,512]{1,0:T(8,128)(2,1)S(1)} all-gather(bf16[32,512]{1,0:T(8,128)(2,1)S(1)} %convolution_convert_fusion.2), channel_id=1, replica_groups=mesh['mode'=8,'member'=16] {'member'}, dimensions={0}, use_global_device_ids=true | all-gather | bytes 557056 | tf_op jit(solution)/shard_map/all_gather | solution.py:36
  35.8 8.2 %fusion = bf16[6144,512]{0,1:T(8,128)(2,1)} fusion(bf16[512,512]{1,0:T(8,128)(2,1)S(1)} %all_gather.3, bf16[6144,512]{1,0:T(8,128)(2,1)} %param.10), kind=kOutput, calls=%fused_computation.1 | convolution fusion | flops 3224371200 | bytes 13107200 | tf_op jit(solution)/shard_map/dot_general | solution.py:37
  44.0 8.7 %copy.14 = bf16[6144,512]{1,0:T(8,128)(2,1)} copy(bf16[6144,512]{0,1:T(8,128)(2,1)} %fusion) | data formatting | bytes 12582912 | tf_op jit(solution)/shard_map/convert_element_type | solution.py:37
  52.7 0.0 copy-start.1
  52.7 0.0 copy-start.2
  52.7 11.5 %reshape.37 = bf16[1024,3072]{1,0:T(8,128)(2,1)} reshape(bf16[6144,512]{1,0:T(8,128)(2,1)} %copy.14) | data formatting | bytes 12582912 | tf_op jit(solution)/shard_map/reshape | solution.py:41
  64.2 0.0 copy-done.1
  64.2 0.0 copy-done.2
  64.2 0.0 copy-start.5
  64.2 0.0 copy-start.3
  64.2 0.0 copy-start.4
  64.3 7.6 %convolution_convert_fusion.1 = bf16[512,3072]{1,0:T(8,128)(2,1)} fusion(bf16[1024,3072]{1,0:T(8,128)(2,1)} %reshape.37, s32[1024]{0:T(1024)S(1)} %bitcast.28), kind=kOutput, calls=%fused_computation.2 | convolution fusion | flops 3223322624 | bytes 9441280 | tf_op jit(solution)/shard_map/dot_general | solution.py:44
  71.8 0.0 reduce-scatter.2.cloned.1.call-update
  71.8 0.0 copy-done.5
  71.9 0.6 dynamic-slice
  73.1 0.0 copy-done.3
  73.1 33.8 %reduce-scatter.2.cloned.1.call-done = bf16[64,3072]{1,0:T(8,128)(2,1)} async-done(((bf16[512,3072]{1,0:T(8,128)(2,1)}), bf16[64,3072]{1,0:T(8,128)(2,1)}) %reduce-scatter.2.cloned.1.call-update) | async-done | bytes 393232 | tf_op jit(solution)/shard_map/reduce_scatter | solution.py:45
  107.0 83.7 %all-reduce.2 = f32[64,3072]{1,0:T(8,128)S(1)} all-reduce(bf16[64,3072]{1,0:T(8,128)(2,1)} %reduce-scatter.2.cloned.1.call-done), channel_id=3, replica_groups=mesh['mode'=8,'member'=16] {'member'}, use_global_device_ids=true, to_apply=%region_1.0.clone | all-reduce | flops 196608 | bytes 1179648
  190.8 0.0 copy-done
  190.8 0.2 fusion.2
  191.0 0.0 copy-done.4
  191.0 0.7 abs_reduce_fusion
  (5 shorter events, 0.1 us)
Async XLA Ops:
  6.5 184.2 %copy-start = (f32[8,6]{1,0:T(8,128)S(1)}, f32[8,6]{1,0:T(8,128)}, u32[]{:S(2)}) copy-start(f32[8,6]{1,0:T(8,128)} %param.14) | copy-start | bytes 580
  6.5 100.4 %reduce-scatter.2.cloned.1.call-start = ((), (), s32[]{:S(2)}) async-start(), calls=%async_computation.1 | async-start | bytes 3538944 | tf_op jit(solution)/shard_map/reduce_scatter | solution.py:45
  52.7 11.5 %copy-start.1 = (s32[1024,1]{0,1:T(1,128)S(1)}, s32[1024,1]{0,1:T(1,128)}, u32[]{:S(2)}) copy-start(s32[1024,1]{0,1:T(1,128)} %param.12) | copy-start | bytes 12292
  52.7 11.5 %copy-start.2 = (s32[1024,1]{0,1:T(1,128)S(1)}, s32[1024,1]{0,1:T(1,128)}, u32[]{:S(2)}) copy-start(s32[1024,1]{0,1:T(1,128)} %param.11) | copy-start | bytes 12292
  64.2 7.6 %copy-start.5 = (u32[128]{0:T(128)S(1)}, u32[128]{0:T(128)}, u32[]{:S(2)}) copy-start(u32[128]{0:T(128)} %constant.11) | copy-start | bytes 1540
  64.2 8.9 %copy-start.3 = (s32[4,8]{1,0:T(4,128)S(1)}, s32[4,8]{1,0:T(4,128)}, u32[]{:S(2)}) copy-start(s32[4,8]{1,0:T(4,128)} %param.13) | copy-start | bytes 388
  64.2 126.7 %copy-start.4 = (f32[4,8]{1,0:T(4,128)S(1)}, f32[4,8]{1,0:T(4,128)}, u32[]{:S(2)}) copy-start(f32[4,8]{1,0:T(4,128)} %param.15) | copy-start | bytes 388
Sparse Core Ops, SparseCore 0:
  72.0 34.9 reduce-scatter.1
where the time goes:
time: 199 us
  blocking collectives  109 us (55%)
  waiting for transfers between devices  33.9 us (17%)
  local copies, waits for them, and re-layouts  24.2 us (12%)
  matrix products  16.2 us (8%)
  between operations  14.2 us (7%)
    unnamed x1, blocking collectives  83.7 us
    reduce_scatter x1, waiting for transfers between devices, local(): lax.psum_scatter(group_part.astype(jnp.bfloat16), 'mode', scatter_dimensi...  33.8 us
    all_gather x1, blocking collectives, local(): modal_resp = lax.all_gather(local_resp, 'member', axis=0, tiled=True)  25.6 us
    reshape x1, local copies, waits for them, and re-layouts, local(): packed = partial.reshape(members_here, comp_count * partial.shape[1])  11.5 us
    convert_element_type x1, local copies, waits for them, and re-layouts, local(): jnp.dot(mode_shapes, modal_resp, preferred_element_type=jnp.float32)  8.68 us
    dot_general x1, matrix products, local(): jnp.dot(mode_shapes, modal_resp, preferred_element_type=jnp.float32)  8.21 us
    dot_general x1, matrix products, local(): group_part = jnp.dot(selector, packed, preferred_element_type=jnp.float32)  7.56 us
  transfers between devices with their start and end apart: 1, of which 1 were waited for; matrix products, arithmetic and copies ran while one was open for 0% of the time, Pallas kernels for 0%

commit v1 on v0

--- a/solution.py
+++ b/solution.py
@@ -33,7 +33,8 @@
     local_resp = lax.dot_general(
         modal_kernel[:, ::-1], lagged, (((1,), (1,)), ((), ())), preferred_element_type=jnp.float32
     ).astype(jnp.bfloat16)
-    modal_resp = lax.all_gather(local_resp, "member", axis=0, tiled=True)
+    row_out = jnp.stack(lax.axis_size("member") * [local_resp], axis=0)
+    modal_resp = jnp.concatenate(lax.all_to_all(row_out, "member", 0, 0), 0)
     partial = jnp.dot(mode_shapes, modal_resp, preferred_element_type=jnp.float32).astype(
         jnp.bfloat16
     )

time: 199 us -> 192 us (0.965)
  blocking collectives: 109 us -> 83.7 us
  waiting for transfers between devices: 33.9 us -> 43.5 us
  starting transfers between devices: 0.01 us -> 8.17 us
    all_gather x1 -> x0, blocking collectives: 25.6 us -> none  [local(): modal_resp = lax.all_gather(local_resp, 'member', axis=0, tiled=True)]
    all_to_all x0 -> x1, waiting for transfers between devices: none -> 11.4 us  [local(): modal_resp = jnp.concatenate(lax.all_to_all(row_out, 'member', 0, 0), 0)]
    all_to_all x0 -> x1, starting transfers between devices: none -> 8.13 us  [local(): modal_resp = jnp.concatenate(lax.all_to_all(row_out, 'member', 0, 0), 0)]
  transfers between devices with their start and end apart: 1 -> 2, of which waited for: 1 -> 2; matrix products, arithmetic and copies ran while one was open for 0% -> 0% of each run, Pallas kernels for 0% -> 0%
where the time goes in v1:
time: 192 us
  blocking collectives  83.7 us (44%)
  waiting for transfers between devices  43.5 us (23%)
  local copies, waits for them, and re-layouts  25.1 us (13%)
  matrix products  16.2 us (8%)
  between operations  14.2 us (7%)
  starting transfers between devices  8.17 us (4%)
    unnamed x1, blocking collectives  83.7 us
    reduce_scatter x1, waiting for transfers between devices, local(): lax.psum_scatter(group_part.astype(jnp.bfloat16), 'mode', scatter_dimensi...  32 us
    reshape x1, local copies, waits for them, and re-layouts, local(): packed = partial.reshape(members_here, comp_count * partial.shape[1])  11.5 us
    all_to_all x1, waiting for transfers between devices, local(): modal_resp = jnp.concatenate(lax.all_to_all(row_out, 'member', 0, 0), 0)  11.4 us
    convert_element_type x1, local copies, waits for them, and re-layouts, local(): jnp.dot(mode_shapes, modal_resp, preferred_element_type=jnp.float32)  8.68 us
    dot_general x1, matrix products, local(): jnp.dot(mode_shapes, modal_resp, preferred_element_type=jnp.float32)  8.19 us
    all_to_all x1, starting transfers between devices, local(): modal_resp = jnp.concatenate(lax.all_to_all(row_out, 'member', 0, 0), 0)  8.13 us
    dot_general x1, matrix products, local(): group_part = jnp.dot(selector, packed, preferred_element_type=jnp.float32)  7.56 us
  transfers between devices with their start and end apart: 2, of which 2 were waited for; matrix products, arithmetic and copies ran while one was open for 0% of the time, Pallas kernels for 0%

profile of v1, /device:TPU:0, one launch (start us, length us, event | category | flops | bytes accessed | tf_op | source)
XLA Modules:
  0.0 191.6 jit_solution(14188243174455018353)
XLA Ops:
  6.5 0.0 copy-start
  6.5 0.0 copy-start.2
  6.5 0.0 copy-start.1
  6.5 0.8 tile.4
  7.3 0.6 tile.10
  8.0 0.2 slice.8
  8.2 0.1 copy.21
  8.3 1.6 rev.3
  10.0 0.2 convolution_convert_fusion.2
  10.2 0.9 stack.2
  11.1 8.1 %all-to-all-start = ((bf16[16,32,512]{2,1,0:T(8,128)(2,1)}), bf16[16,32,512]{2,1,0:T(8,128)(2,1)S(1)}, u32[]{:S(2)}, u32[]{:S(2)}) async-start(bf16[16,32,512]{2,1,0:T(8,128)(2,1)} %stack.2), calls=%async_computation | async-start | bytes 1048576 | tf_op jit(solution)/shard_map/all_to_all | solution.py:37
  19.2 0.0 reduce-scatter.2.cloned.1.call-start
  19.3 0.0 copy-done.2
  19.3 0.0 copy-done.1
  19.3 11.4 %all-to-all-done = bf16[16,32,512]{2,1,0:T(8,128)(2,1)S(1)} async-done(((bf16[16,32,512]{2,1,0:T(8,128)(2,1)}), bf16[16,32,512]{2,1,0:T(8,128)(2,1)S(1)}, u32[]{:S(2)}, u32[]{:S(2)}) %all-to-all-start) | async-done | bytes 524320 | tf_op jit(solution)/shard_map/all_to_all | solution.py:37
  30.8 8.2 %fusion = bf16[6144,512]{0,1:T(8,128)(2,1)} fusion(bf16[512,512]{1,0:T(8,128)(2,1)S(1)} %bitcast.29, bf16[6144,512]{1,0:T(8,128)(2,1)} %param.10), kind=kOutput, calls=%fused_computation.1 | convolution fusion | flops 3224371200 | bytes 13107200 | tf_op jit(solution)/shard_map/dot_general | solution.py:38
  39.0 8.7 %copy.14 = bf16[6144,512]{1,0:T(8,128)(2,1)} copy(bf16[6144,512]{0,1:T(8,128)(2,1)} %fusion) | data formatting | bytes 12582912 | tf_op jit(solution)/shard_map/convert_element_type | solution.py:38
  47.6 11.5 %reshape.43 = bf16[1024,3072]{1,0:T(8,128)(2,1)} reshape(bf16[6144,512]{1,0:T(8,128)(2,1)} %copy.14) | data formatting | bytes 12582912 | tf_op jit(solution)/shard_map/reshape | solution.py:42
  59.1 0.0 copy-start.5
  59.1 0.0 copy-start.3
  59.1 0.0 copy-start.4
  59.1 7.6 %convolution_convert_fusion.1 = bf16[512,3072]{1,0:T(8,128)(2,1)} fusion(bf16[1024,3072]{1,0:T(8,128)(2,1)} %reshape.43, s32[1024]{0:T(1024)S(1)} %bitcast.30), kind=kOutput, calls=%fused_computation.2 | convolution fusion | flops 3223322624 | bytes 9441280 | tf_op jit(solution)/shard_map/dot_general | solution.py:45
  66.7 0.0 reduce-scatter.2.cloned.1.call-update
  66.7 0.0 copy-done.5
  66.7 0.6 dynamic-slice
  67.9 0.0 copy-done.3
  68.0 32.0 %reduce-scatter.2.cloned.1.call-done = bf16[64,3072]{1,0:T(8,128)(2,1)} async-done(((bf16[512,3072]{1,0:T(8,128)(2,1)}), bf16[64,3072]{1,0:T(8,128)(2,1)}) %reduce-scatter.2.cloned.1.call-update) | async-done | bytes 393232 | tf_op jit(solution)/shard_map/reduce_scatter | solution.py:46
  100.0 83.7 %all-reduce.2 = f32[64,3072]{1,0:T(8,128)S(1)} all-reduce(bf16[64,3072]{1,0:T(8,128)(2,1)} %reduce-scatter.2.cloned.1.call-done), channel_id=3, replica_groups=mesh['mode'=8,'member'=16] {'member'}, use_global_device_ids=true, to_apply=%region_1.0.clone | all-reduce | flops 196608 | bytes 1179648
  183.8 0.0 copy-done
  183.8 0.2 fusion.2
  184.0 0.0 copy-done.4
  184.0 0.7 abs_reduce_fusion
  (5 shorter events, 0.1 us)
Async XLA Ops:
  6.5 177.2 %copy-start = (f32[8,6]{1,0:T(8,128)S(1)}, f32[8,6]{1,0:T(8,128)}, u32[]{:S(2)}) copy-start(f32[8,6]{1,0:T(8,128)} %param.14) | copy-start | bytes 580
  6.5 12.7 %copy-start.2 = (s32[1024,1]{0,1:T(1,128)S(1)}, s32[1024,1]{0,1:T(1,128)}, u32[]{:S(2)}) copy-start(s32[1024,1]{0,1:T(1,128)} %param.11) | copy-start | bytes 12292
  6.5 12.8 %copy-start.1 = (s32[1024,1]{0,1:T(1,128)S(1)}, s32[1024,1]{0,1:T(1,128)}, u32[]{:S(2)}) copy-start(s32[1024,1]{0,1:T(1,128)} %param.12) | copy-start | bytes 12292
  11.1 19.7 %all-to-all-start = ((bf16[16,32,512]{2,1,0:T(8,128)(2,1)}), bf16[16,32,512]{2,1,0:T(8,128)(2,1)S(1)}, u32[]{:S(2)}, u32[]{:S(2)}) async-start(bf16[16,32,512]{2,1,0:T(8,128)(2,1)} %stack.2), calls=%async_computation | async-start | bytes 1048576 | tf_op jit(solution)/shard_map/all_to_all | solution.py:37
  19.2 80.8 %reduce-scatter.2.cloned.1.call-start = ((), (), s32[]{:S(2)}) async-start(), calls=%async_computation.2 | async-start | bytes 3538944 | tf_op jit(solution)/shard_map/reduce_scatter | solution.py:46
  59.1 7.6 %copy-start.5 = (u32[128]{0:T(128)S(1)}, u32[128]{0:T(128)}, u32[]{:S(2)}) copy-start(u32[128]{0:T(128)} %constant.11) | copy-start | bytes 1540
  59.1 8.8 %copy-start.3 = (s32[4,8]{1,0:T(4,128)S(1)}, s32[4,8]{1,0:T(4,128)}, u32[]{:S(2)}) copy-start(s32[4,8]{1,0:T(4,128)} %param.13) | copy-start | bytes 388
  59.1 124.9 %copy-start.4 = (f32[4,8]{1,0:T(4,128)S(1)}, f32[4,8]{1,0:T(4,128)}, u32[]{:S(2)}) copy-start(f32[4,8]{1,0:T(4,128)} %param.15) | copy-start | bytes 388
Sparse Core Ops, SparseCore 0:
  66.8 33.1 reduce-scatter.1
